TPU v7x, 32 devices: a whole 2x2x4 slice. The times are simulated.
32 devices in a mesh: groups: 2 (over x), wide: 16 (over z, y, core).
Axes of the slice: x: 2, y: 2, z: 4, core: 2. Of those that a mesh axis runs over, the one named last changes fastest.
Arguments:
- activity: bfloat16 [1024, 16, 512], P(('groups', 'wide')), parts along dimension 0, may hold values from -6 to 6
- grad_out: bfloat16 [1024, 16, 512], P('groups', 'wide'), parts along dimension 0, may hold values from -6 to 6
- spatial_weights: bfloat16 [512, 2048], replicated, may hold values from -8 to 8
- temporal_weights: bfloat16 [512, 2048], replicated, may hold values from -8 to 8
- spatial_gain: float32 [512], replicated, may hold values from 0.25 to 1.75
- temporal_gain: float32 [512], replicated, may hold values from 0.25 to 1.75
- adjacency: int32 [16, 16], replicated, may hold values from 0 to 1
- channel_count: int32 [8], P('groups'), parts along dimension 0, may hold values from 128 to 2048
- session_id: int32 [1024], P('groups'), parts along dimension 0, may hold values from 0 to 3, never falling along the last dimension, each value on 1 to 256 neighbouring positions
Outputs:
- layer_out: bfloat16 [1024, 16, 512], P('groups', 'wide'), parts along dimension 0
- grad_activity: bfloat16 [1024, 16, 512], P(('groups', 'wide')), parts along dimension 0
- spatial_grad: float32 [1024, 2048], P(('groups', 'wide')), parts along dimension 0
- temporal_grad: float32 [1024, 2048], P(('groups', 'wide')), parts along dimension 0
There are 2 independent parts, one for each index of `groups`. A program takes and returns all parts, laid end to end along the dimension named above; an argument that names none is the same for every part. Nothing has to cross between parts.
Inputs may be any that keep to these rules, and one draw needn't show every extreme that they name: `session_id`: session ids never fall along time; every session holds 1 to 256 bins, one exactly 256.
All inputs are finite; a program needn't handle non-finite values.
Results may differ from a plain program's by a relative error of at most 0.015.
Values may be sent and summed in bfloat16 or wider, within the bound.
No kernel may reach another device: no remote copies, remote signals or barrier semaphores. Data moves between devices by JAX's collectives and lax.ppermute only.
A program may use at most 192 MiB of HBM per device.

v0:
```python
import jax
import jax.numpy as jnp
from jax import lax
from jax.sharding import PartitionSpec as P

HEADS = 8
eps_norm = 1e-05
block_channels = 128


def norm_inverse(rows):
    values = rows.astype(jnp.float32)
    return lax.rsqrt(jnp.mean(values * values, axis=-1, keepdims=True) + eps_norm)


def norm_forward(rows, gain):
    inverse = norm_inverse(rows)
    return ((rows.astype(jnp.float32) * inverse * gain).astype(jnp.bfloat16), inverse)


def norm_backward(rows, gain, inverse, grad_normed):
    values = rows.astype(jnp.float32)
    scaled = grad_normed * gain
    inner = jnp.mean(values * scaled, axis=-1, keepdims=True)
    return inverse * scaled - values * inverse * inverse * inverse * inner


def normalized_affinity(asking_vectors, lookup_array, admissible_pairs, sharpness_divisor):
    unnormalized_affinities = (
        jnp.einsum(
            "...uo,...ao->...ua", asking_vectors, lookup_array, preferred_element_type=jnp.float32
        )
        * sharpness_divisor
    )
    unnormalized_affinities = jnp.where(admissible_pairs, unnormalized_affinities, -1e30)
    row_max = jnp.max(unnormalized_affinities, axis=-1, keepdims=True)
    expo = jnp.exp(unnormalized_affinities - row_max)
    return expo / jnp.sum(expo, axis=-1, keepdims=True)


def compute_affinity_outputs(
    asking_vectors, lookup_array, payload_array, admissible_pairs, sharpness_divisor
):
    truncated_outcome = normalized_affinity(
        asking_vectors, lookup_array, admissible_pairs, sharpness_divisor
    ).astype(jnp.bfloat16)
    return jnp.einsum(
        "...qk,...kd->...qd", truncated_outcome, payload_array, preferred_element_type=jnp.float32
    ).astype(jnp.bfloat16)


def compute_affinity_derivatives(
    asking_vectors,
    lookup_array,
    payload_array,
    admissible_pairs,
    sharpness_divisor,
    combined_output,
    blended_output_derivative,
):
    coefficient_array = normalized_affinity(
        asking_vectors, lookup_array, admissible_pairs, sharpness_divisor
    )
    truncated_outcome = coefficient_array.astype(jnp.bfloat16)
    grad_values = jnp.einsum(
        "...qk,...qd->...kd",
        truncated_outcome,
        blended_output_derivative,
        preferred_element_type=jnp.float32,
    )
    coefficient_derivative = jnp.einsum(
        "...uo,...ao->...ua",
        blended_output_derivative,
        payload_array,
        preferred_element_type=jnp.float32,
    )
    paired_inner_sums = jnp.sum(
        blended_output_derivative.astype(jnp.float32) * combined_output.astype(jnp.float32),
        axis=-1,
        keepdims=True,
    )
    affinity_derivative = (
        coefficient_array * (coefficient_derivative - paired_inner_sums) * sharpness_divisor
    ).astype(jnp.bfloat16)
    grad_queries = jnp.einsum(
        "...qk,...kd->...qd", affinity_derivative, lookup_array, preferred_element_type=jnp.float32
    )
    grad_keys = jnp.einsum(
        "...qk,...qd->...kd",
        affinity_derivative,
        asking_vectors,
        preferred_element_type=jnp.float32,
    )
    return (
        grad_queries.astype(jnp.bfloat16),
        grad_keys.astype(jnp.bfloat16),
        grad_values.astype(jnp.bfloat16),
    )


def temporal_split(projected):
    pieces = projected.reshape(projected.shape[0], 3, HEADS, projected.shape[1] // (3 * HEADS))
    return [pieces[:, index].transpose(1, 0, 2) for index in range(3)]


def temporal_forward(projected, admissible_pairs):
    asking_vectors, lookup_array, payload_array = temporal_split(projected)
    sharpness_divisor = float(asking_vectors.shape[-1]) ** (-0.5)
    combined_output = compute_affinity_outputs(
        asking_vectors, lookup_array, payload_array, admissible_pairs[None], sharpness_divisor
    )
    return combined_output.transpose(1, 0, 2).reshape(projected.shape[0], -1)


def temporal_backward(projected, admissible_pairs, combined_output, blended_output_derivative):
    asking_vectors, lookup_array, payload_array = temporal_split(projected)
    sharpness_divisor = float(asking_vectors.shape[-1]) ** (-0.5)
    bins = projected.shape[0]
    subspace_outputs = combined_output.reshape(bins, HEADS, -1).transpose(1, 0, 2)
    subspace_derivative = blended_output_derivative.reshape(bins, HEADS, -1).transpose(1, 0, 2)
    derivative_collection = compute_affinity_derivatives(
        asking_vectors,
        lookup_array,
        payload_array,
        admissible_pairs[None],
        sharpness_divisor,
        subspace_outputs,
        subspace_derivative,
    )
    return jnp.stack(derivative_collection, axis=0).transpose(2, 0, 1, 3).reshape(bins, -1)


def spatial_split(projected):
    pieces = projected.reshape(
        projected.shape[0], projected.shape[1], 3, HEADS, projected.shape[2] // (3 * HEADS)
    )
    return [pieces[:, :, index].transpose(0, 2, 1, 3) for index in range(3)]


def spatial_forward(projected, admissible_pairs):
    asking_vectors, lookup_array, payload_array = spatial_split(projected)
    sharpness_divisor = float(asking_vectors.shape[-1]) ** (-0.5)
    combined_output = compute_affinity_outputs(
        asking_vectors, lookup_array, payload_array, admissible_pairs, sharpness_divisor
    )
    return combined_output.transpose(0, 2, 1, 3).reshape(projected.shape[0], projected.shape[1], -1)


def spatial_backward(projected, admissible_pairs, combined_output, blended_output_derivative):
    asking_vectors, lookup_array, payload_array = spatial_split(projected)
    sharpness_divisor = float(asking_vectors.shape[-1]) ** (-0.5)
    bins, blocks = (projected.shape[0], projected.shape[1])
    subspace_outputs = combined_output.reshape(bins, blocks, HEADS, -1).transpose(0, 2, 1, 3)
    subspace_derivative = blended_output_derivative.reshape(bins, blocks, HEADS, -1).transpose(
        0, 2, 1, 3
    )
    derivative_collection = compute_affinity_derivatives(
        asking_vectors,
        lookup_array,
        payload_array,
        admissible_pairs,
        sharpness_divisor,
        subspace_outputs,
        subspace_derivative,
    )
    return (
        jnp.stack(derivative_collection, axis=0).transpose(1, 3, 0, 2, 4).reshape(bins, blocks, -1)
    )


def spatial_allowed(sessions_here, channel_count, adjacency):
    block_count = adjacency.shape[0]
    block_ids = jnp.arange(block_count, dtype=jnp.int32)
    session_pick = (
        sessions_here[:, None] == jnp.arange(channel_count.shape[0], dtype=jnp.int32)[None, :]
    ).astype(jnp.int32)
    count_rows = jnp.sum(session_pick * channel_count[None, :], axis=1)
    live_block = block_ids[None, :] * block_channels < count_rows[:, None]
    linked = adjacency > 0
    itself = block_ids[:, None] == block_ids[None, :]
    admissible_pairs = linked[None, :, :] & live_block[:, None, :] | itself[None, :, :]
    return admissible_pairs[:, None, :, :]


def project(rows, coefficient_array):
    return jnp.einsum("tbd,de->tbe", rows, coefficient_array, preferred_element_type=jnp.float32)


def project_back(derivative_collection, coefficient_array):
    return jnp.einsum(
        "tbe,de->tbd", derivative_collection, coefficient_array, preferred_element_type=jnp.float32
    )


def weight_term(left, right):
    return jnp.einsum("tbd,tbe->de", left, right, preferred_element_type=jnp.float32)


def per_device(
    activity,
    grad_out,
    spatial_weights,
    temporal_weights,
    spatial_gain,
    temporal_gain,
    adjacency,
    channel_count,
    session_id,
):
    local_bins = activity.shape[0]
    model_width = activity.shape[2]
    first_bin = lax.axis_index("wide") * local_bins
    sessions_here = lax.dynamic_slice_in_dim(session_id, first_bin, local_bins)
    normed_one, inverse_one = norm_forward(activity, spatial_gain)
    spatial_proj = project(normed_one, spatial_weights[:, : 3 * model_width]).astype(jnp.bfloat16)
    allowed_space = spatial_allowed(sessions_here, channel_count, adjacency)
    spatial_context = spatial_forward(spatial_proj, allowed_space)
    middle = (
        activity.astype(jnp.float32)
        + project(spatial_context, spatial_weights[:, 3 * model_width :])
    ).astype(jnp.bfloat16)
    middle_block = lax.all_to_all(middle, "wide", split_axis=1, concat_axis=0, tiled=True)
    normed_two, inverse_two = norm_forward(middle_block, temporal_gain)
    temporal_proj = project(normed_two, temporal_weights[:, : 3 * model_width]).astype(jnp.bfloat16)
    allowed_time = session_id[:, None] == session_id[None, :]
    by_block = jnp.moveaxis(temporal_proj, 1, 0)
    temporal_context = jnp.moveaxis(
        lax.map(lambda block_rows: temporal_forward(block_rows, allowed_time), by_block), 0, 1
    )
    layer_out = (
        middle_block.astype(jnp.float32)
        + project(temporal_context, temporal_weights[:, 3 * model_width :])
    ).astype(jnp.bfloat16)
    grad_temporal_context = project_back(grad_out, temporal_weights[:, 3 * model_width :]).astype(
        jnp.bfloat16
    )
    stacked = (
        by_block,
        jnp.moveaxis(temporal_context, 1, 0),
        jnp.moveaxis(grad_temporal_context, 1, 0),
    )
    grad_temporal_proj = jnp.moveaxis(
        lax.map(
            lambda items: temporal_backward(items[0], allowed_time, items[1], items[2]), stacked
        ),
        0,
        1,
    )
    grad_normed_two = project_back(grad_temporal_proj, temporal_weights[:, : 3 * model_width])
    grad_middle = (
        grad_out.astype(jnp.float32)
        + norm_backward(middle_block, temporal_gain, inverse_two, grad_normed_two)
    ).astype(jnp.bfloat16)
    grad_middle_time = lax.all_to_all(grad_middle, "wide", split_axis=0, concat_axis=1, tiled=True)
    normed_cols = normed_two
    context_cols = temporal_context
    temporal_grad = lax.psum_scatter(
        jnp.concatenate(
            [weight_term(normed_cols, grad_temporal_proj), weight_term(context_cols, grad_out)],
            axis=1,
        ).astype(jnp.bfloat16),
        "wide",
        scatter_dimension=0,
        tiled=True,
    ).astype(jnp.float32)
    grad_spatial_context = project_back(
        grad_middle_time, spatial_weights[:, 3 * model_width :]
    ).astype(jnp.bfloat16)
    grad_spatial_proj = spatial_backward(
        spatial_proj, allowed_space, spatial_context, grad_spatial_context
    )
    grad_normed_one = project_back(grad_spatial_proj, spatial_weights[:, : 3 * model_width])
    grad_activity = (
        grad_middle_time.astype(jnp.float32)
        + norm_backward(activity, spatial_gain, inverse_one, grad_normed_one)
    ).astype(jnp.bfloat16)
    normed_cols = normed_one
    context_cols = spatial_context
    spatial_grad = lax.psum_scatter(
        jnp.concatenate(
            [
                weight_term(normed_cols, grad_spatial_proj),
                weight_term(context_cols, grad_middle_time),
            ],
            axis=1,
        ).astype(jnp.bfloat16),
        "wide",
        scatter_dimension=0,
        tiled=True,
    ).astype(jnp.float32)
    return (layer_out, grad_activity, spatial_grad, temporal_grad)


def solution(mesh):
    placed = (
        P(("groups", "wide"), None, None),
        P("groups", "wide", None),
        P(),
        P(),
        P(),
        P(),
        P(),
        P("groups"),
        P("groups"),
    )
    return jax.shard_map(
        per_device,
        mesh=mesh,
        in_specs=placed,
        out_specs=(
            P("groups", "wide", None),
            P(("groups", "wide"), None, None),
            P(("groups", "wide"), None),
            P(("groups", "wide"), None),
        ),
        check_vma=False,
    )
```

profile of v0, /device:TPU:0, one launch (start us, length us, event | category | flops | bytes accessed | tf_op | source)
XLA Modules:
  0.0 230.5 jit_solution(11808287719107655246)
XLA Ops:
  7.2 1.2 fusion.41
  8.4 3.8 %convolution_convert_fusion.2 = bf16[32,16,1536]{2,1,0:T(8,128)(2,1)} fusion(bf16[512,2048]{1,0:T(8,128)(2,1)} %param.11, bf16[32,16,512]{2,1,0:T(8,128)(2,1)} %param.9, f32[512]{0:T(512)} %param.13, f32[32,16]{1,0:T(8,128)S(1)} %add_rsqrt_fusion), kind=kOutput, calls=%fused_computation.15 | convolution fusion | flops 807141376 | bytes 3674112 | tf_op jit(solution)/shard_map/tbd,de->tbe/dot_general | solution.py:186
  12.2 4.0 %reshape.297 = bf16[32,16,3,8,64]{4,3,2,1,0:T(8,128)(2,1)S(1)} reshape(bf16[32,16,1536]{2,1,0:T(8,128)(2,1)} %convolution_convert_fusion.2) | data formatting | bytes 3145728 | tf_op jit(solution)/shard_map/reshape | solution.py:134
  16.2 2.1 fusion.82
  18.9 4.3 %fusion.83 = (f32[32,8,16]{2,1,0:T(8,128)S(1)}, f32[32,8,16,16]{2,3,1,0:T(8,128)}) fusion(pred[32,16,16]{1,2,0:T(8,128)(4,1)S(1)} %and_or_fusion, bf16[32,16,1,8,64]{4,3,2,1,0:T(8,128)(2,1)} %get-tuple-element.29, bf16[32,16,1,8,64]{4,3,2,1,0:T(8,128)(2,1)} %get-tuple-element.28), kind=kOutput, calls=%fused_computation.131 | convolution fusion | flops 8650767 | bytes 1335296 | tf_op jit(solution)/shard_map/sub | solution.py:37
  23.1 2.2 convolution_convert_fusion.6
  25.3 1.0 copy-done.7
  26.6 0.6 reshape.298
  27.2 1.7 fusion.26
  28.9 1.1 copy.98
  30.0 7.4 %all-to-all-start = ((bf16[32,16,512]{2,0,1:T(8,128)(2,1)}), bf16[32,16,512]{2,0,1:T(8,128)(2,1)S(1)}, u32[]{:S(2)}, u32[]{:S(2)}) async-start(bf16[32,16,512]{2,0,1:T(8,128)(2,1)} %copy.98), calls=%async_computation | async-start | bytes 1048576 | tf_op jit(solution)/shard_map/all_to_all | solution.py:222
  37.4 1.0 copy.104
  38.6 2.3 %convolution_convert_fusion.13 = bf16[512,512]{0,1:T(8,128)(2,1)} fusion(bf16[512,1,512]{2,0,1:T(8,128)(2,1)S(1)} %copy-done.11, bf16[512,2048]{1,0:T(8,128)(2,1)} %param.12), kind=kOutput, calls=%fused_computation.54 | convolution fusion | flops 268697600 | bytes 1572864 | tf_op jit(solution)/shard_map/tbe,de->tbd/dot_general | solution.py:190
  40.9 10.9 %all-to-all-done = bf16[32,16,512]{2,0,1:T(8,128)(2,1)S(1)} async-done(((bf16[32,16,512]{2,0,1:T(8,128)(2,1)}), bf16[32,16,512]{2,0,1:T(8,128)(2,1)S(1)}, u32[]{:S(2)}, u32[]{:S(2)}) %all-to-all-start) | async-done | bytes 524320 | tf_op jit(solution)/shard_map/all_to_all | solution.py:222
  52.0 0.3 copy.101
  52.7 0.6 copy-done.9
  53.3 3.7 %convolution_convert_fusion.1 = bf16[512,1536]{1,0:T(8,128)(2,1)} fusion(bf16[512,2048]{1,0:T(8,128)(2,1)} %param.12, f32[512,512]{0,1:T(8,128)S(1)} %copy.101, f32[512]{0:T(512)S(1)} %copy-done.26, f32[512]{0:T(512)S(1)} %rsqrt.21), kind=kOutput, calls=%fused_computation.14 | convolution fusion | flops 806879232 | bytes 4198400 | tf_op jit(solution)/shard_map/tbd,de->tbe/dot_general | solution.py:186
  57.0 1.7 copy.102
  58.7 5.4 %fusion.84 = (f32[8,512]{1,0:T(8,128)S(1)}, f32[8,512,512]{1,2,0:T(8,128)}) fusion(pred[512,512]{0,1:T(8,128)(4,1)S(1)} %broadcast_compare_fusion, bf16[512,3,8,64]{0,3,2,1:T(8,128)(2,1)S(1)} %bitcast.171), kind=kOutput, calls=%fused_computation.132 | convolution fusion | flops 276824576 | bytes 9715712 | tf_op jit(solution)/shard_map/while/body/eval_jaxpr/sub | solution.py:37
  64.1 4.7 %fusion.6 = bf16[8,512,512]{1,2,0:T(8,128)(2,1)S(1)} fusion(f32[8,512,512]{1,2,0:T(8,128)} %get-tuple-element.40, f32[8,512]{1,0:T(8,128)S(1)} %get-tuple-element.33), kind=kLoop, calls=%fused_computation.10 | loop fusion | flops 4194304 | bytes 12599296 | tf_op jit(solution)/shard_map/while/body/eval_jaxpr/convert_element_type | solution.py:46
  68.8 0.8 multiply_reduce_fusion.2
  69.6 1.4 fusion.33
  71.0 1.4 copy-done.2
  72.3 1.8 multiply_convert_fusion
  74.1 1.4 fusion.32
  75.5 0.8 fusion.34
  76.5 1.2 copy-done.10
  77.8 1.0 copy-done.23
  78.8 1.0 multiply_reduce_fusion.1
  79.8 1.1 fusion.45
  81.0 0.5 broadcast.200
  81.5 2.1 reduce.6
  83.8 1.2 reshape.314
  85.0 4.1 %all-to-all-start.1 = ((bf16[16,2,8192]{2,1,0:T(2,128)(2,1)}), bf16[16,2,8192]{2,1,0:T(2,128)(2,1)S(1)}, u32[]{:S(2)}, u32[]{:S(2)}) async-start(bf16[16,2,8192]{2,1,0:T(2,128)(2,1)} %reshape.314), calls=%async_computation.1 | async-start | bytes 1048576 | tf_op jit(solution)/shard_map/all_to_all | solution.py:254
  89.4 0.4 convolution_convert_fusion.9
  89.9 2.6 %convolution_convert_fusion = bf16[512,1536]{1,0:T(8,128)(2,1)S(1)} fusion(bf16[512,1536]{0,1:T(8,128)(2,1)} %bitcast.182, f32[512,1,1,1,1,1,512]{6,0,5,4,3,2,1:T(8,128)S(1)} %bitcast.169, f32[512]{0:T(512)S(1)} %copy-done.26, f32[512]{0:T(512)S(1)} %rsqrt.21), kind=kOutput, calls=%fused_computation.13 | convolution fusion | flops 806879232 | bytes 4198400 | tf_op jit(solution)/shard_map/tbd,tbe->de/dot_general | solution.py:196
  92.5 1.6 pad_maximum_fusion.1
  94.1 9.4 %all-to-all-done.1 = bf16[16,2,8192]{2,1,0:T(2,128)(2,1)S(1)} async-done(((bf16[16,2,8192]{2,1,0:T(2,128)(2,1)}), bf16[16,2,8192]{2,1,0:T(2,128)(2,1)S(1)}, u32[]{:S(2)}, u32[]{:S(2)}) %all-to-all-start.1) | async-done | bytes 524320 | tf_op jit(solution)/shard_map/all_to_all | solution.py:254
  103.6 0.5 reshape.315
  104.1 0.9 copy.129
  105.0 2.6 %convolution_convert_fusion.10 = bf16[32,16,512]{2,1,0:T(8,128)(2,1)} fusion(bf16[512,2048]{1,0:T(8,128)(2,1)} %param.11, bf16[16,32,1,512]{3,1,0,2:T(8,128)(2,1)} %bitcast.56), kind=kOutput, calls=%fused_computation.51 | convolution fusion | flops 268697600 | bytes 1572864 | tf_op jit(solution)/shard_map/tbe,de->tbd/dot_general | solution.py:190
  107.6 1.7 reshape.304
  109.4 0.6 multiply_reduce_fusion
  110.0 1.0 copy-done.29
  111.0 0.7 multiply_convert_fusion.1
  111.8 0.5 copy-done.6
  112.3 0.5 fusion.20
  112.8 0.7 copy-done.5
  113.5 0.7 fusion.21
  114.2 0.7 fusion.22
  114.9 0.8 maximum_bitcast_fusion
  115.7 0.8 copy.115
  116.5 3.0 %reshape.305 = bf16[32,16,1536]{2,1,0:T(8,128)(2,1)} reshape(bf16[32,16,3,8,64]{4,3,2,1,0:T(8,128)(2,1)S(1)} %copy.115) | data formatting | bytes 3145728 | tf_op jit(solution)/shard_map/reshape | solution.py:167
  119.5 1.9 fusion.28
  121.5 1.1 fusion.7
  122.6 1.6 pad_maximum_fusion
  124.2 1.2 copy-done.1
  125.5 2.4 %fusion.31 = bf16[512,1,512]{2,0,1:T(8,128)(2,1)} fusion(f32[512,512]{1,0:T(8,128)S(1)} %bitcast.170, bf16[512,512]{0,1:T(8,128)(2,1)S(1)} %bitcast.177, bf16[512,2048]{1,0:T(8,128)(2,1)} %param.12), kind=kOutput, calls=%fused_computation.60 | convolution fusion | flops 268959744 | bytes 2621440 | tf_op jit(solution)/shard_map/tbd,de->tbe/dot_general | solution.py:186
  127.9 2.5 %fusion.42 = (f32[32,16]{1,0:T(8,128)S(1)}, f32[32,16,512]{2,1,0:T(8,128)S(1)}) fusion(bf16[32,16,512]{2,1,0:T(8,128)(2,1)S(1)} %copy-done.14, f32[512]{0:T(512)S(1)} %copy-done.27, bf16[32,16,1536]{2,1,0:T(8,128)(2,1)S(1)} %copy-done.19, bf16[512,2048]{1,0:T(8,128)(2,1)} %param.11), kind=kOutput, calls=%fused_computation.71 | convolution fusion | flops 806354432 | bytes 4722688 | tf_op jit(solution)/shard_map/tbe,de->tbd/dot_general | solution.py:190
  130.4 2.3 %fusion.40 = bf16[32,16,512]{2,1,0:T(8,128)(2,1)} fusion(bf16[32,16,512]{2,1,0:T(8,128)(2,1)S(1)} %copy-done.14, f32[32,16,512]{2,1,0:T(8,128)S(1)} %get-tuple-element.46, f32[32,16]{1,0:T(8,128)S(1)} %broadcast_multiply_fusion, f32[32,16]{1,0:T(8,128)S(1)} %add_rsqrt_fusion, bf16[16,32,1,512]{3,1,0,2:T(8,128)(2,1)} %bitcast.56), kind=kLoop, calls=%fused_computation.69 | loop fusion | flops 2621440 | bytes 2625536 | tf_op jit(solution)/shard_map/convert_element_type | solution.py:276
  132.8 24.4 %reduce-scatter.5.cloned.1.call-done = bf16[32,2048]{1,0:T(8,128)(2,1)} async-done(((bf16[512,2048]{1,0:T(8,128)(2,1)}), bf16[32,2048]{1,0:T(8,128)(2,1)}) %reduce-scatter.5.cloned.1.call-update) | async-done | bytes 131088 | tf_op jit(solution)/shard_map/reduce_scatter | solution.py:257
  157.2 1.6 convert_element_type.231
  158.8 63.2 %reduce-scatter.3.cloned.1.call-done = bf16[32,2048]{1,0:T(8,128)(2,1)} async-done(((bf16[512,2048]{1,0:T(8,128)(2,1)}), bf16[32,2048]{1,0:T(8,128)(2,1)}) %reduce-scatter.3.cloned.1.call-update) | async-done | bytes 131088 | tf_op jit(solution)/shard_map/reduce_scatter | solution.py:279
  222.0 1.6 convert_element_type.226
  (76 shorter events, 2.5 us)
Async XLA Ops:
  16.2 2.2 copy-start.25
  16.2 2.2 copy-start.24
  16.2 2.3 %copy-start.28 = (s32[4]{0:T(128)S(1)}, s32[4]{0:T(128)}, u32[]{:S(2)}) copy-start(s32[4]{0:T(128)} %param.16) | copy-start | bytes 52
  18.8 4.3 %copy-start.20 = (bf16[32,16,1,8,64]{4,3,2,1,0:T(8,128)(2,1)S(1)}, bf16[32,16,1,8,64]{4,3,2,1,0:T(8,128)(2,1)}, u32[]{:S(2)}) copy-start(bf16[32,16,1,8,64]{4,3,2,1,0:T(8,128)(2,1)} %get-tuple-element.30) | copy-start | bytes 1572868
  25.3 1.0 copy-start.7
  25.3 1.9 copy-start.13
  27.2 2.8 %copy-start.22 = (bf16[32,16,512]{2,1,0:T(8,128)(2,1)}, bf16[32,16,512]{2,1,0:T(8,128)(2,1)S(1)}, u32[]{:S(2)}) copy-start(bf16[32,16,512]{2,1,0:T(8,128)(2,1)S(1)} %reshape.298) | copy-start | bytes 1572868
  27.2 10.2 %copy-start.11 = (bf16[512,1,512]{2,0,1:T(8,128)(2,1)S(1)}, bf16[512,1,512]{2,0,1:T(8,128)(2,1)}, u32[]{:S(2)}) copy-start(bf16[512,1,512]{2,0,1:T(8,128)(2,1)} %param.10) | copy-start | bytes 1572868
  30.0 21.9 %all-to-all-start = ((bf16[32,16,512]{2,0,1:T(8,128)(2,1)}), bf16[32,16,512]{2,0,1:T(8,128)(2,1)S(1)}, u32[]{:S(2)}, u32[]{:S(2)}) async-start(bf16[32,16,512]{2,0,1:T(8,128)(2,1)} %copy.98), calls=%async_computation | async-start | bytes 1048576 | tf_op jit(solution)/shard_map/all_to_all | solution.py:222
  40.9 12.4 %copy-start.26 = (f32[512]{0:T(512)S(1)}, f32[512]{0:T(512)}, u32[]{:S(2)}) copy-start(f32[512]{0:T(512)} %param.14) | copy-start | bytes 6148
  52.0 37.9 %copy-start = (f32[32,16,512]{2,0,1:T(8,128)}, f32[32,16,512]{2,0,1:T(8,128)S(1)}, u32[]{:S(2)}) copy-start(f32[32,16,512]{2,0,1:T(8,128)S(1)} %convert_element_type.236) | copy-start | bytes 3145732
  52.3 1.0 copy-start.9
  64.1 4.7 %copy-start.16 = (bf16[512,512]{0,1:T(8,128)(2,1)S(1)}, bf16[512,512]{0,1:T(8,128)(2,1)}, u32[]{:S(2)}) copy-start(bf16[512,512]{0,1:T(8,128)(2,1)} %convolution_convert_fusion.13) | copy-start | bytes 1572868
  68.8 3.6 %copy-start.2 = (f32[8,512,512]{1,2,0:T(8,128)S(1)}, f32[8,512,512]{1,2,0:T(8,128)}, u32[]{:S(2)}) copy-start(f32[8,512,512]{1,2,0:T(8,128)} %get-tuple-element.40) | copy-start | bytes 25165828
  69.6 19.8 %copy-start.3 = (bf16[8,512,64]{1,2,0:T(8,128)(2,1)}, bf16[8,512,64]{1,2,0:T(8,128)(2,1)S(1)}, u32[]{:S(2)}) copy-start(bf16[8,512,64]{1,2,0:T(8,128)(2,1)S(1)} %get-tuple-element.42) | copy-start | bytes 1572868
  76.3 1.5 copy-start.10
  76.3 2.5 %copy-start.23 = (bf16[512,2048]{1,0:T(8,128)(2,1)S(1)}, bf16[512,2048]{1,0:T(8,128)(2,1)}, u32[]{:S(2)}) copy-start(bf16[512,2048]{1,0:T(8,128)(2,1)} %param.12) | copy-start | bytes 6291460
  76.5 3.3 %copy-start.17 = (bf16[3,8,512,64]{2,3,1,0:T(8,128)(2,1)}, bf16[3,8,512,64]{2,3,1,0:T(8,128)(2,1)S(1)}, u32[]{:S(2)}) copy-start(bf16[3,8,512,64]{2,3,1,0:T(8,128)(2,1)S(1)} %pad_maximum_fusion.2) | copy-start | bytes 4718596
  78.8 1.0 copy-start.15
  81.5 7.9 %copy-start.12 = (bf16[512,1,512]{2,0,1:T(8,128)(2,1)S(1)}, bf16[512,1,512]{2,0,1:T(8,128)(2,1)}, u32[]{:S(2)}) copy-start(bf16[512,1,512]{2,0,1:T(8,128)(2,1)} %param.10) | copy-start | bytes 1572868
  85.0 18.6 %all-to-all-start.1 = ((bf16[16,2,8192]{2,1,0:T(2,128)(2,1)}), bf16[16,2,8192]{2,1,0:T(2,128)(2,1)S(1)}, u32[]{:S(2)}, u32[]{:S(2)}) async-start(bf16[16,2,8192]{2,1,0:T(2,128)(2,1)} %reshape.314), calls=%async_computation.1 | async-start | bytes 1048576 | tf_op jit(solution)/shard_map/all_to_all | solution.py:254
  89.1 68.1 %reduce-scatter.5.cloned.1.call-start = ((), (), s32[]{:S(2)}) async-start(), calls=%async_computation.5 | async-start | bytes 2228224 | tf_op jit(solution)/shard_map/reduce_scatter | solution.py:257
  94.1 127.9 %reduce-scatter.3.cloned.1.call-start = ((), (), s32[]{:S(2)}) async-start(), calls=%async_computation.4 | async-start | bytes 2228224 | tf_op jit(solution)/shard_map/reduce_scatter | solution.py:279
  105.0 4.3 %copy-start.8 = (bf16[32,8,16,64]{3,2,1,0:T(8,128)(2,1)S(1)}, bf16[32,8,16,64]{3,2,1,0:T(8,128)(2,1)}, u32[]{:S(2)}) copy-start(bf16[32,8,16,64]{3,2,1,0:T(8,128)(2,1)} %copy-done.7) | copy-start | bytes 1572868
  107.6 2.4 %copy-start.21 = (bf16[32,16,1,8,64]{4,3,2,1,0:T(8,128)(2,1)S(1)}, bf16[32,16,1,8,64]{4,3,2,1,0:T(8,128)(2,1)}, u32[]{:S(2)}) copy-start(bf16[32,16,1,8,64]{4,3,2,1,0:T(8,128)(2,1)} %get-tuple-element.30) | copy-start | bytes 1572868
  109.4 1.6 copy-start.29
  111.0 1.2 copy-start.6
  112.3 1.2 copy-start.5
  119.5 1.9 copy-start.14
  119.5 2.0 copy-start.18
  119.5 2.0 copy-start.27
  124.1 1.2 copy-start.1
  124.1 1.4 copy-start.4
  125.5 2.4 %copy-start.19 = (bf16[32,16,1536]{2,1,0:T(8,128)(2,1)S(1)}, bf16[32,16,1536]{2,1,0:T(8,128)(2,1)}, u32[]{:S(2)}) copy-start(bf16[32,16,1536]{2,1,0:T(8,128)(2,1)} %reshape.305) | copy-start | bytes 4718596
Sparse Core Ops, SparseCore 0:
  94.2 62.9 reduce-scatter.4
  161.4 60.6 reduce-scatter.2
where the time goes:
time: 232 us; the launch traced here: 230 us
  waiting for transfers between devices  108 us (47%)
  matrix products  46.6 us (20%)
  local copies, waits for them, and re-layouts  29.2 us (13%)
  other arithmetic  20.3 us (9%)
  between operations  14.6 us (6%)
  starting transfers between devices  11.8 us (5%)
    reduce_scatter x1, waiting for transfers between devices, per_device(): lax.psum_scatter(jnp.concatenate([weight_term(normed_cols, grad_spatial_p...  63.2 us
    reduce_scatter x1, waiting for transfers between devices, per_device(): lax.psum_scatter(jnp.concatenate([weight_term(normed_cols, grad_temporal_...  24.4 us
    unnamed x66, local copies, waits for them, and re-layouts  12.8 us
    dot_general x4, matrix products, project(): jnp.einsum('tbd,de->tbe', rows, coefficient_array, preferred_element_type...  11.6 us
    all_to_all x1, waiting for transfers between devices, per_device(): lax.all_to_all(middle, 'wide', split_axis=1, concat_axis=0, tiled=True)  10.9 us
    sub x2, matrix products, normalized_affinity(): expo = jnp.exp(unnormalized_affinities - row_max)  9.67 us
    all_to_all x1, waiting for transfers between devices, per_device(): lax.all_to_all(grad_middle, 'wide', split_axis=0, concat_axis=1, tiled=True)  9.45 us
    dot_general x4, matrix products, project_back(): jnp.einsum('tbe,de->tbd', derivative_collection, coefficient_array, prefe...  8.39 us
  transfers between devices with their start and end apart: 4, of which 4 were waited for; matrix products, arithmetic and copies ran while one was open for 15% of the time, Pallas kernels for 0%

commit v1 on v0

--- a/solution.py
+++ b/solution.py
@@ -6,6 +6,43 @@
 HEADS = 8
 eps_norm = 1e-05
 block_channels = 128
+
+
+def fill_pages_by_axis(unit, dimension_no, mine):
+    everything = unit.shape
+    kept_arr = unit.reshape(
+        *everything[:dimension_no],
+        mine,
+        everything[dimension_no] // mine,
+        *everything[dimension_no + 1 :]
+    )
+    x_now = jnp.moveaxis(kept_arr, dimension_no, 0)
+    return x_now
+
+
+def put_trees(u_in, at_axis):
+    u_in = jnp.moveaxis(u_in, 0, at_axis)
+    value_now = u_in.shape
+    v1 = u_in.reshape(
+        *value_now[:at_axis], value_now[at_axis] * value_now[at_axis + 1], *value_now[at_axis + 2 :]
+    )
+    return v1
+
+
+def fill_the_results(arr_in, a_name, mine_x, x_local):
+    carry = lax.axis_size(a_name)
+    val2 = lax.axis_index(a_name)
+    b_now, built = (carry, val2)
+    arr_out = fill_pages_by_axis(arr_in, mine_x, b_now)
+    history = [arr_out[built]]
+    for pp in range(1, b_now):
+        latest = arr_out[built ^ pp]
+        raw_out = lax.ppermute(latest, a_name, [(m, m ^ pp) for m in range(b_now)])
+        history.append(raw_out)
+    outcome_arr = jnp.stack(history)
+    arr_out = outcome_arr[built ^ jnp.arange(b_now)]
+    after = put_trees(arr_out, x_local)
+    return after
 
 
 def norm_inverse(rows):
@@ -219,7 +256,7 @@
         activity.astype(jnp.float32)
         + project(spatial_context, spatial_weights[:, 3 * model_width :])
     ).astype(jnp.bfloat16)
-    middle_block = lax.all_to_all(middle, "wide", split_axis=1, concat_axis=0, tiled=True)
+    middle_block = fill_the_results(middle, "wide", 1, 0)
     normed_two, inverse_two = norm_forward(middle_block, temporal_gain)
     temporal_proj = project(normed_two, temporal_weights[:, : 3 * model_width]).astype(jnp.bfloat16)
     allowed_time = session_id[:, None] == session_id[None, :]

time: 232 us -> 270 us (1.16)
  waiting for transfers between devices: 108 us -> 143 us
  starting transfers between devices: 11.8 us -> 20.3 us
  matrix products: 46.6 us -> 42 us
    ppermute x0 -> x15, waiting for transfers between devices: none -> 44.7 us  [fill_the_results(): raw_out = lax.ppermute(latest, a_name, [(m, m ^ pp) for m in range(b_now)])]
    ppermute x0 -> x15, starting transfers between devices: none -> 16.6 us  [fill_the_results(): raw_out = lax.ppermute(latest, a_name, [(m, m ^ pp) for m in range(b_now)])]
    all_to_all x1 -> x0, waiting for transfers between devices: 10.9 us -> none  [per_device(): lax.all_to_all(middle, 'wide', split_axis=1, concat_axis=0, tiled=True)]
    all_to_all x1 -> x0, starting transfers between devices: 7.39 us -> none  [per_device(): lax.all_to_all(middle, 'wide', split_axis=1, concat_axis=0, tiled=True)]
    unnamed x66 -> x80, local copies, waits for them, and re-layouts: 12.8 us -> 13.3 us
  transfers between devices with their start and end apart: 4 -> 18, of which waited for: 4 -> 13; matrix products, arithmetic and copies ran while one was open for 15% -> 11% of each run, Pallas kernels for 0% -> 0%
where the time goes in v1:
time: 270 us; the launch traced here: 269 us
  waiting for transfers between devices  143 us (53%)
  matrix products  42 us (16%)
  local copies, waits for them, and re-layouts  30.4 us (11%)
  starting transfers between devices  20.3 us (8%)
  other arithmetic  18.3 us (7%)
  between operations  14.9 us (6%)
    reduce_scatter x1, waiting for transfers between devices, per_device(): lax.psum_scatter(jnp.concatenate([weight_term(normed_cols, grad_spatial_p...  63.2 us
    ppermute x15, waiting for transfers between devices, fill_the_results(): raw_out = lax.ppermute(latest, a_name, [(m, m ^ pp) for m in range(b_now)])  44.7 us
    reduce_scatter x1, waiting for transfers between devices, per_device(): lax.psum_scatter(jnp.concatenate([weight_term(normed_cols, grad_temporal_...  25.3 us
    ppermute x15, starting transfers between devices, fill_the_results(): raw_out = lax.ppermute(latest, a_name, [(m, m ^ pp) for m in range(b_now)])  16.6 us
    unnamed x80, local copies, waits for them, and re-layouts  13.3 us
    dot_general x4, matrix products, project(): jnp.einsum('tbd,de->tbe', rows, coefficient_array, preferred_element_type...  11.4 us
    all_to_all x1, waiting for transfers between devices, per_device(): lax.all_to_all(grad_middle, 'wide', split_axis=0, concat_axis=1, tiled=True)  9.75 us
    sub x2, matrix products, normalized_affinity(): expo = jnp.exp(unnormalized_affinities - row_max)  8.35 us
  transfers between devices with their start and end apart: 18, of which 13 were waited for; matrix products, arithmetic and copies ran while one was open for 11% of the time, Pallas kernels for 0%

profile of v1, /device:TPU:0, one launch (start us, length us, event | category | flops | bytes accessed | tf_op | source)
XLA Modules:
  0.0 268.8 jit_solution(14773185842125897377)
XLA Ops:
  8.0 1.2 fusion.41
  9.3 3.8 %convolution_convert_fusion.2 = bf16[32,16,1536]{2,1,0:T(8,128)(2,1)} fusion(bf16[512,2048]{1,0:T(8,128)(2,1)} %param.11, bf16[32,16,512]{2,1,0:T(8,128)(2,1)} %param.9, f32[512]{0:T(512)} %param.13, f32[32,16]{1,0:T(8,128)S(1)} %add_rsqrt_fusion), kind=kOutput, calls=%fused_computation.16 | convolution fusion | flops 807141376 | bytes 3674112 | tf_op jit(solution)/shard_map/tbd,de->tbe/dot_general | solution.py:223
  13.1 4.0 %reshape.381 = bf16[32,16,3,8,64]{4,3,2,1,0:T(8,128)(2,1)S(1)} reshape(bf16[32,16,1536]{2,1,0:T(8,128)(2,1)} %convolution_convert_fusion.2) | data formatting | bytes 3145728 | tf_op jit(solution)/shard_map/reshape | solution.py:171
  17.1 2.1 fusion.82
  19.6 2.9 %fusion.83 = (f32[32,8,16]{2,1,0:T(8,128)S(1)}, f32[32,8,16,16]{2,3,1,0:T(8,128)S(1)}) fusion(pred[32,16,16]{1,2,0:T(8,128)(4,1)S(1)} %and_or_fusion, bf16[32,16,1,8,64]{4,3,2,1,0:T(8,128)(2,1)} %get-tuple-element.29, bf16[32,16,1,8,64]{4,3,2,1,0:T(8,128)(2,1)} %get-tuple-element.28), kind=kOutput, calls=%fused_computation.167 | convolution fusion | flops 8650767 | bytes 1335296 | tf_op jit(solution)/shard_map/sub | solution.py:74
  22.6 1.4 copy-done.27
  24.5 0.9 copy-done.5
  26.4 1.7 fusion.26
  28.1 1.5 constant_dynamic-slice_fusion
  29.7 5.5 %collective-permute-start.14 = (bf16[32,1,512]{2,1,0:T(2,128)(2,1)S(1)}, bf16[32,1,512]{2,1,0:T(2,128)(2,1)S(1)}, u32[]{:S(2)}, u32[]{:S(2)}) collective-permute-start(bf16[32,1,512]{2,1,0:T(2,128)(2,1)S(1)} %get-tuple-element.31), channel_id=1, source_target_pairs={{0,15},{1,14},{2,13},{3,12},{4,11},{5,10},{6,9},{7,8},{8,7},{9,6},... | collective-permute-start | bytes 98312 | tf_op jit(solution)/shard_map/ppermute | solution.py:40
  35.8 3.1 %collective-permute-start.12 = (bf16[32,1,512]{2,1,0:T(2,128)(2,1)S(1)}, bf16[32,1,512]{2,1,0:T(2,128)(2,1)S(1)}, u32[]{:S(2)}, u32[]{:S(2)}) collective-permute-start(bf16[32,1,512]{2,1,0:T(2,128)(2,1)S(1)} %get-tuple-element.33), channel_id=1, source_target_pairs={{0,13},{1,12},{2,15},{3,14},{4,9},{5,8},{6,11},{7,10},{8,5},{9,4},... | collective-permute-start | bytes 98312 | tf_op jit(solution)/shard_map/ppermute | solution.py:40
  39.8 2.3 convolution_convert_fusion.13
  42.1 1.3 collective-permute-start.1
  43.4 3.1 %collective-permute-done.1 = bf16[32,1,512]{2,1,0:T(2,128)(2,1)S(1)} collective-permute-done((bf16[32,1,512]{2,1,0:T(2,128)(2,1)S(1)}, bf16[32,1,512]{2,1,0:T(2,128)(2,1)S(1)}, u32[]{:S(2)}, u32[]{:S(2)}) %collective-permute-start.1) | collective-permute-done | bytes 32800 | tf_op jit(solution)/shard_map/ppermute | solution.py:40
  46.5 0.8 collective-permute-start.2
  47.2 3.6 %collective-permute-done.2 = bf16[32,1,512]{2,1,0:T(2,128)(2,1)S(1)} collective-permute-done((bf16[32,1,512]{2,1,0:T(2,128)(2,1)S(1)}, bf16[32,1,512]{2,1,0:T(2,128)(2,1)S(1)}, u32[]{:S(2)}, u32[]{:S(2)}) %collective-permute-start.2) | collective-permute-done | bytes 32800 | tf_op jit(solution)/shard_map/ppermute | solution.py:40
  50.9 4.3 %collective-permute-done.3 = bf16[32,1,512]{2,1,0:T(2,128)(2,1)S(1)} collective-permute-done((bf16[32,1,512]{2,1,0:T(2,128)(2,1)S(1)}, bf16[32,1,512]{2,1,0:T(2,128)(2,1)S(1)}, u32[]{:S(2)}, u32[]{:S(2)}) %collective-permute-start.3) | collective-permute-done | bytes 32800 | tf_op jit(solution)/shard_map/ppermute | solution.py:40
  55.1 3.7 %collective-permute-done.4 = bf16[32,1,512]{2,1,0:T(2,128)(2,1)S(1)} collective-permute-done((bf16[32,1,512]{2,1,0:T(2,128)(2,1)S(1)}, bf16[32,1,512]{2,1,0:T(2,128)(2,1)S(1)}, u32[]{:S(2)}, u32[]{:S(2)}) %collective-permute-start.4) | collective-permute-done | bytes 32800 | tf_op jit(solution)/shard_map/ppermute | solution.py:40
  58.8 1.0 collective-permute-start.5
  59.9 4.1 %collective-permute-done.5 = bf16[32,1,512]{2,1,0:T(2,128)(2,1)S(1)} collective-permute-done((bf16[32,1,512]{2,1,0:T(2,128)(2,1)S(1)}, bf16[32,1,512]{2,1,0:T(2,128)(2,1)S(1)}, u32[]{:S(2)}, u32[]{:S(2)}) %collective-permute-start.5) | collective-permute-done | bytes 32800 | tf_op jit(solution)/shard_map/ppermute | solution.py:40
  64.2 4.4 %collective-permute-done.6 = bf16[32,1,512]{2,1,0:T(2,128)(2,1)S(1)} collective-permute-done((bf16[32,1,512]{2,1,0:T(2,128)(2,1)S(1)}, bf16[32,1,512]{2,1,0:T(2,128)(2,1)S(1)}, u32[]{:S(2)}, u32[]{:S(2)}) %collective-permute-start.6) | collective-permute-done | bytes 32800 | tf_op jit(solution)/shard_map/ppermute | solution.py:40
  68.6 3.0 %collective-permute-start.7 = (bf16[32,1,512]{2,1,0:T(2,128)(2,1)S(1)}, bf16[32,1,512]{2,1,0:T(2,128)(2,1)S(1)}, u32[]{:S(2)}, u32[]{:S(2)}) collective-permute-start(bf16[32,1,512]{2,1,0:T(2,128)(2,1)S(1)} %get-tuple-element.44), channel_id=1, source_target_pairs={{0,8},{1,9},{2,10},{3,11},{4,12},{5,13},{6,14},{7,15},{8,0},{9,1},... | collective-permute-start | bytes 98312 | tf_op jit(solution)/shard_map/ppermute | solution.py:40
  71.6 3.8 %collective-permute-done.7 = bf16[32,1,512]{2,1,0:T(2,128)(2,1)S(1)} collective-permute-done((bf16[32,1,512]{2,1,0:T(2,128)(2,1)S(1)}, bf16[32,1,512]{2,1,0:T(2,128)(2,1)S(1)}, u32[]{:S(2)}, u32[]{:S(2)}) %collective-permute-start.7) | collective-permute-done | bytes 32800 | tf_op jit(solution)/shard_map/ppermute | solution.py:40
  75.4 6.2 %collective-permute-done.8 = bf16[32,1,512]{2,1,0:T(2,128)(2,1)S(1)} collective-permute-done((bf16[32,1,512]{2,1,0:T(2,128)(2,1)S(1)}, bf16[32,1,512]{2,1,0:T(2,128)(2,1)S(1)}, u32[]{:S(2)}, u32[]{:S(2)}) %collective-permute-start.8) | collective-permute-done | bytes 32800 | tf_op jit(solution)/shard_map/ppermute | solution.py:40
  82.0 5.6 %collective-permute-done.9 = bf16[32,1,512]{2,1,0:T(2,128)(2,1)S(1)} collective-permute-done((bf16[32,1,512]{2,1,0:T(2,128)(2,1)S(1)}, bf16[32,1,512]{2,1,0:T(2,128)(2,1)S(1)}, u32[]{:S(2)}, u32[]{:S(2)}) %collective-permute-start.9) | collective-permute-done | bytes 32800 | tf_op jit(solution)/shard_map/ppermute | solution.py:40
  87.6 6.0 %collective-permute-done.10 = bf16[32,1,512]{2,1,0:T(2,128)(2,1)S(1)} collective-permute-done((bf16[32,1,512]{2,1,0:T(2,128)(2,1)S(1)}, bf16[32,1,512]{2,1,0:T(2,128)(2,1)S(1)}, u32[]{:S(2)}, u32[]{:S(2)}) %collective-permute-start.10) | collective-permute-done | bytes 32800 | tf_op jit(solution)/shard_map/ppermute | solution.py:40
  94.8 3.6 %convolution_convert_fusion.1 = bf16[512,1536]{1,0:T(8,128)(2,1)} fusion(bf16[512,512]{1,0:T(8,128)(2,1)S(1)} %multiply_convert_fusion.3, bf16[512,2048]{1,0:T(8,128)(2,1)} %param.12), kind=kOutput, calls=%fused_computation.15 | convolution fusion | flops 806092800 | bytes 3670016 | tf_op jit(solution)/shard_map/tbd,de->tbe/dot_general | solution.py:223
  98.4 1.7 copy.471
  100.1 5.4 %fusion.84 = (f32[8,512]{1,0:T(8,128)S(1)}, f32[8,512,512]{1,2,0:T(8,128)}) fusion(pred[512,512]{0,1:T(8,128)(4,1)S(1)} %broadcast_compare_fusion, bf16[512,3,8,64]{0,3,2,1:T(8,128)(2,1)S(1)} %bitcast.205), kind=kOutput, calls=%fused_computation.168 | convolution fusion | flops 276824576 | bytes 9715712 | tf_op jit(solution)/shard_map/while/body/eval_jaxpr/sub | solution.py:74
  105.5 4.7 %fusion.6 = bf16[8,512,512]{1,2,0:T(8,128)(2,1)S(1)} fusion(f32[8,512,512]{1,2,0:T(8,128)} %get-tuple-element.56, f32[8,512]{1,0:T(8,128)S(1)} %get-tuple-element.55), kind=kLoop, calls=%fused_computation.11 | loop fusion | flops 4194304 | bytes 12599296 | tf_op jit(solution)/shard_map/while/body/eval_jaxpr/convert_element_type | solution.py:83
  110.2 0.8 multiply_reduce_fusion.2
  111.0 1.4 fusion.33
  112.4 1.4 copy-done
  113.8 1.8 multiply_convert_fusion
  115.6 1.4 fusion.32
  117.0 0.8 fusion.34
  118.0 2.0 copy-done.22
  120.0 1.1 fusion.46
  122.0 1.0 reduce.5
  123.0 1.2 reshape.412
  124.2 3.6 %all-to-all-start = ((bf16[16,2,8192]{2,1,0:T(2,128)(2,1)}), bf16[16,2,8192]{2,1,0:T(2,128)(2,1)S(1)}, u32[]{:S(2)}, u32[]{:S(2)}) async-start(bf16[16,2,8192]{2,1,0:T(2,128)(2,1)} %reshape.412), calls=%async_computation | async-start | bytes 1048576 | tf_op jit(solution)/shard_map/all_to_all | solution.py:291
  129.6 1.2 convolution_convert_fusion
  130.8 1.6 pad_maximum_fusion.1
  132.5 9.8 %all-to-all-done = bf16[16,2,8192]{2,1,0:T(2,128)(2,1)S(1)} async-done(((bf16[16,2,8192]{2,1,0:T(2,128)(2,1)}), bf16[16,2,8192]{2,1,0:T(2,128)(2,1)S(1)}, u32[]{:S(2)}, u32[]{:S(2)}) %all-to-all-start) | async-done | bytes 524320 | tf_op jit(solution)/shard_map/all_to_all | solution.py:291
  142.9 0.8 copy-done.10
  143.7 2.3 convolution_convert_fusion.10
  146.1 1.7 reshape.388
  148.5 1.0 copy-done.28
  149.5 0.7 multiply_convert_fusion.1
  151.3 0.7 copy-done.3
  153.4 0.8 maximum_bitcast_fusion
  154.1 0.8 copy.483
  155.0 3.0 %reshape.389 = bf16[32,16,1536]{2,1,0:T(8,128)(2,1)} reshape(bf16[32,16,3,8,64]{4,3,2,1,0:T(8,128)(2,1)S(1)} %copy.483) | data formatting | bytes 3145728 | tf_op jit(solution)/shard_map/reshape | solution.py:204
  157.9 1.9 fusion.28
  159.9 1.1 fusion.7
  161.0 1.6 pad_maximum_fusion
  162.6 1.0 copy-done.2
  164.0 2.3 fusion.31
  166.3 2.6 fusion.42
  168.9 1.3 fusion.40
  170.2 25.3 %reduce-scatter.5.cloned.1.call-done = bf16[32,2048]{1,0:T(8,128)(2,1)} async-done(((bf16[512,2048]{1,0:T(8,128)(2,1)}), bf16[32,2048]{1,0:T(8,128)(2,1)}) %reduce-scatter.5.cloned.1.call-update) | async-done | bytes 131088 | tf_op jit(solution)/shard_map/reduce_scatter | solution.py:294
  195.5 1.6 convert_element_type.225
  197.1 63.2 %reduce-scatter.3.cloned.1.call-done = bf16[32,2048]{1,0:T(8,128)(2,1)} async-done(((bf16[512,2048]{1,0:T(8,128)(2,1)}), bf16[32,2048]{1,0:T(8,128)(2,1)}) %reduce-scatter.3.cloned.1.call-update) | async-done | bytes 131088 | tf_op jit(solution)/shard_map/reduce_scatter | solution.py:316
  260.3 1.6 convert_element_type.220
  (121 shorter events, 12.9 us)
Async XLA Ops:
  17.1 2.2 copy-start.23
  17.1 2.2 copy-start.26
  19.6 4.3 %copy-start.19 = (bf16[32,16,1,8,64]{4,3,2,1,0:T(8,128)(2,1)S(1)}, bf16[32,16,1,8,64]{4,3,2,1,0:T(8,128)(2,1)}, u32[]{:S(2)}) copy-start(bf16[32,16,1,8,64]{4,3,2,1,0:T(8,128)(2,1)} %get-tuple-element.30) | copy-start | bytes 1572868
  22.6 1.4 copy-start.27
  22.6 1.9 copy-start.29
  24.5 1.0 copy-start.5
  24.5 1.8 copy-start.12
  26.4 3.3 %copy-start.21 = (bf16[32,16,512]{2,1,0:T(8,128)(2,1)}, bf16[32,16,512]{2,1,0:T(8,128)(2,1)S(1)}, u32[]{:S(2)}) copy-start(bf16[32,16,512]{2,1,0:T(8,128)(2,1)S(1)} %reshape.382) | copy-start | bytes 1572868
  26.4 13.4 %copy-start.9 = (bf16[512,1,512]{2,0,1:T(8,128)(2,1)S(1)}, bf16[512,1,512]{2,0,1:T(8,128)(2,1)}, u32[]{:S(2)}) copy-start(bf16[512,1,512]{2,0,1:T(8,128)(2,1)} %param.10) | copy-start | bytes 1572868
  29.7 64.0 %collective-permute-start.14 = (bf16[32,1,512]{2,1,0:T(2,128)(2,1)S(1)}, bf16[32,1,512]{2,1,0:T(2,128)(2,1)S(1)}, u32[]{:S(2)}, u32[]{:S(2)}) collective-permute-start(bf16[32,1,512]{2,1,0:T(2,128)(2,1)S(1)} %get-tuple-element.31), channel_id=1, source_target_pairs={{0,15},{1,14},{2,13},{3,12},{4,11},{5,10},{6,9},{7,8},{8,7},{9,6},... | collective-permute-start | bytes 98312 | tf_op jit(solution)/shard_map/ppermute | solution.py:40
  35.2 58.5 %collective-permute-start.13 = (bf16[32,1,512]{2,1,0:T(2,128)(2,1)S(1)}, bf16[32,1,512]{2,1,0:T(2,128)(2,1)S(1)}, u32[]{:S(2)}, u32[]{:S(2)}) collective-permute-start(bf16[32,1,512]{2,1,0:T(2,128)(2,1)S(1)} %get-tuple-element.32), channel_id=1, source_target_pairs={{0,14},{1,15},{2,12},{3,13},{4,10},{5,11},{6,8},{7,9},{8,6},{9,7},... | collective-permute-start | bytes 98312 | tf_op jit(solution)/shard_map/ppermute | solution.py:40
  35.8 57.8 %collective-permute-start.12 = (bf16[32,1,512]{2,1,0:T(2,128)(2,1)S(1)}, bf16[32,1,512]{2,1,0:T(2,128)(2,1)S(1)}, u32[]{:S(2)}, u32[]{:S(2)}) collective-permute-start(bf16[32,1,512]{2,1,0:T(2,128)(2,1)S(1)} %get-tuple-element.33), channel_id=1, source_target_pairs={{0,13},{1,12},{2,15},{3,14},{4,9},{5,8},{6,11},{7,10},{8,5},{9,4},... | collective-permute-start | bytes 98312 | tf_op jit(solution)/shard_map/ppermute | solution.py:40
  39.0 54.7 %collective-permute-start.11 = (bf16[32,1,512]{2,1,0:T(2,128)(2,1)S(1)}, bf16[32,1,512]{2,1,0:T(2,128)(2,1)S(1)}, u32[]{:S(2)}, u32[]{:S(2)}) collective-permute-start(bf16[32,1,512]{2,1,0:T(2,128)(2,1)S(1)} %get-tuple-element.40), channel_id=1, source_target_pairs={{0,12},{1,13},{2,14},{3,15},{4,8},{5,9},{6,10},{7,11},{8,4},{9,5},... | collective-permute-start | bytes 98312 | tf_op jit(solution)/shard_map/ppermute | solution.py:40
  39.3 2.8 %collective-permute-start = (bf16[32,1,512]{2,1,0:T(2,128)(2,1)S(1)}, bf16[32,1,512]{2,1,0:T(2,128)(2,1)S(1)}, u32[]{:S(2)}, u32[]{:S(2)}) collective-permute-start(bf16[32,1,512]{2,1,0:T(2,128)(2,1)S(1)} %get-tuple-element.51), channel_id=1, source_target_pairs={{0,1},{1,0},{2,3},{3,2},{4,5},{5,4},{6,7},{7,6},{8,9},{9,8},{10,11... | collective-permute-start | bytes 98312 | tf_op jit(solution)/shard_map/ppermute | solution.py:40
  39.8 54.9 %copy-start.24 = (f32[512]{0:T(512)S(1)}, f32[512]{0:T(512)}, u32[]{:S(2)}) copy-start(f32[512]{0:T(512)} %param.14) | copy-start | bytes 6148
  42.1 4.4 %collective-permute-start.1 = (bf16[32,1,512]{2,1,0:T(2,128)(2,1)S(1)}, bf16[32,1,512]{2,1,0:T(2,128)(2,1)S(1)}, u32[]{:S(2)}, u32[]{:S(2)}) collective-permute-start(bf16[32,1,512]{2,1,0:T(2,128)(2,1)S(1)} %get-tuple-element.50), channel_id=1, source_target_pairs={{0,2},{1,3},{2,0},{3,1},{4,6},{5,7},{6,4},{7,5},{8,10},{9,11},{10,... | collective-permute-start | bytes 98312 | tf_op jit(solution)/shard_map/ppermute | solution.py:40
  46.5 4.4 %collective-permute-start.2 = (bf16[32,1,512]{2,1,0:T(2,128)(2,1)S(1)}, bf16[32,1,512]{2,1,0:T(2,128)(2,1)S(1)}, u32[]{:S(2)}, u32[]{:S(2)}) collective-permute-start(bf16[32,1,512]{2,1,0:T(2,128)(2,1)S(1)} %get-tuple-element.49), channel_id=1, source_target_pairs={{0,3},{1,2},{2,1},{3,0},{4,7},{5,6},{6,5},{7,4},{8,11},{9,10},{10,... | collective-permute-start | bytes 98312 | tf_op jit(solution)/shard_map/ppermute | solution.py:40
  50.9 4.3 %collective-permute-start.3 = (bf16[32,1,512]{2,1,0:T(2,128)(2,1)S(1)}, bf16[32,1,512]{2,1,0:T(2,128)(2,1)S(1)}, u32[]{:S(2)}, u32[]{:S(2)}) collective-permute-start(bf16[32,1,512]{2,1,0:T(2,128)(2,1)S(1)} %get-tuple-element.48), channel_id=1, source_target_pairs={{0,4},{1,5},{2,6},{3,7},{4,0},{5,1},{6,2},{7,3},{8,12},{9,13},{10,... | collective-permute-start | bytes 98312 | tf_op jit(solution)/shard_map/ppermute | solution.py:40
  55.1 3.7 %collective-permute-start.4 = (bf16[32,1,512]{2,1,0:T(2,128)(2,1)S(1)}, bf16[32,1,512]{2,1,0:T(2,128)(2,1)S(1)}, u32[]{:S(2)}, u32[]{:S(2)}) collective-permute-start(bf16[32,1,512]{2,1,0:T(2,128)(2,1)S(1)} %get-tuple-element.47), channel_id=1, source_target_pairs={{0,5},{1,4},{2,7},{3,6},{4,1},{5,0},{6,3},{7,2},{8,13},{9,12},{10,... | collective-permute-start | bytes 98312 | tf_op jit(solution)/shard_map/ppermute | solution.py:40
  58.8 5.2 %collective-permute-start.5 = (bf16[32,1,512]{2,1,0:T(2,128)(2,1)S(1)}, bf16[32,1,512]{2,1,0:T(2,128)(2,1)S(1)}, u32[]{:S(2)}, u32[]{:S(2)}) collective-permute-start(bf16[32,1,512]{2,1,0:T(2,128)(2,1)S(1)} %get-tuple-element.46), channel_id=1, source_target_pairs={{0,6},{1,7},{2,4},{3,5},{4,2},{5,3},{6,0},{7,1},{8,14},{9,15},{10,... | collective-permute-start | bytes 98312 | tf_op jit(solution)/shard_map/ppermute | solution.py:40
  64.0 4.6 %collective-permute-start.6 = (bf16[32,1,512]{2,1,0:T(2,128)(2,1)S(1)}, bf16[32,1,512]{2,1,0:T(2,128)(2,1)S(1)}, u32[]{:S(2)}, u32[]{:S(2)}) collective-permute-start(bf16[32,1,512]{2,1,0:T(2,128)(2,1)S(1)} %get-tuple-element.45), channel_id=1, source_target_pairs={{0,7},{1,6},{2,5},{3,4},{4,3},{5,2},{6,1},{7,0},{8,15},{9,14},{10,... | collective-permute-start | bytes 98312 | tf_op jit(solution)/shard_map/ppermute | solution.py:40
  68.6 6.8 %collective-permute-start.7 = (bf16[32,1,512]{2,1,0:T(2,128)(2,1)S(1)}, bf16[32,1,512]{2,1,0:T(2,128)(2,1)S(1)}, u32[]{:S(2)}, u32[]{:S(2)}) collective-permute-start(bf16[32,1,512]{2,1,0:T(2,128)(2,1)S(1)} %get-tuple-element.44), channel_id=1, source_target_pairs={{0,8},{1,9},{2,10},{3,11},{4,12},{5,13},{6,14},{7,15},{8,0},{9,1},... | collective-permute-start | bytes 98312 | tf_op jit(solution)/shard_map/ppermute | solution.py:40
  75.3 6.2 %collective-permute-start.8 = (bf16[32,1,512]{2,1,0:T(2,128)(2,1)S(1)}, bf16[32,1,512]{2,1,0:T(2,128)(2,1)S(1)}, u32[]{:S(2)}, u32[]{:S(2)}) collective-permute-start(bf16[32,1,512]{2,1,0:T(2,128)(2,1)S(1)} %get-tuple-element.43), channel_id=1, source_target_pairs={{0,9},{1,8},{2,11},{3,10},{4,13},{5,12},{6,15},{7,14},{8,1},{9,0},... | collective-permute-start | bytes 98312 | tf_op jit(solution)/shard_map/ppermute | solution.py:40
  81.5 6.1 %collective-permute-start.9 = (bf16[32,1,512]{2,1,0:T(2,128)(2,1)S(1)}, bf16[32,1,512]{2,1,0:T(2,128)(2,1)S(1)}, u32[]{:S(2)}, u32[]{:S(2)}) collective-permute-start(bf16[32,1,512]{2,1,0:T(2,128)(2,1)S(1)} %get-tuple-element.42), channel_id=1, source_target_pairs={{0,10},{1,11},{2,8},{3,9},{4,14},{5,15},{6,12},{7,13},{8,2},{9,3},... | collective-permute-start | bytes 98312 | tf_op jit(solution)/shard_map/ppermute | solution.py:40
  87.6 6.0 %collective-permute-start.10 = (bf16[32,1,512]{2,1,0:T(2,128)(2,1)S(1)}, bf16[32,1,512]{2,1,0:T(2,128)(2,1)S(1)}, u32[]{:S(2)}, u32[]{:S(2)}) collective-permute-start(bf16[32,1,512]{2,1,0:T(2,128)(2,1)S(1)} %get-tuple-element.41), channel_id=1, source_target_pairs={{0,11},{1,10},{2,9},{3,8},{4,15},{5,14},{6,13},{7,12},{8,3},{9,2},... | collective-permute-start | bytes 98312 | tf_op jit(solution)/shard_map/ppermute | solution.py:40
  105.5 4.7 %copy-start.14 = (bf16[512,512]{0,1:T(8,128)(2,1)S(1)}, bf16[512,512]{0,1:T(8,128)(2,1)}, u32[]{:S(2)}) copy-start(bf16[512,512]{0,1:T(8,128)(2,1)} %convolution_convert_fusion.13) | copy-start | bytes 1572868
  110.2 3.6 %copy-start = (f32[8,512,512]{1,2,0:T(8,128)S(1)}, f32[8,512,512]{1,2,0:T(8,128)}, u32[]{:S(2)}) copy-start(f32[8,512,512]{1,2,0:T(8,128)} %get-tuple-element.56) | copy-start | bytes 25165828
  111.0 17.0 %copy-start.1 = (bf16[8,512,64]{1,2,0:T(8,128)(2,1)}, bf16[8,512,64]{1,2,0:T(8,128)(2,1)S(1)}, u32[]{:S(2)}) copy-start(bf16[8,512,64]{1,2,0:T(8,128)(2,1)S(1)} %get-tuple-element.58) | copy-start | bytes 1572868
  117.8 2.2 copy-start.22
  118.0 3.1 %copy-start.15 = (bf16[3,8,512,64]{2,3,1,0:T(8,128)(2,1)}, bf16[3,8,512,64]{2,3,1,0:T(8,128)(2,1)S(1)}, u32[]{:S(2)}) copy-start(bf16[3,8,512,64]{2,3,1,0:T(8,128)(2,1)S(1)} %pad_maximum_fusion.2) | copy-start | bytes 4718596
  124.2 18.1 %all-to-all-start = ((bf16[16,2,8192]{2,1,0:T(2,128)(2,1)}), bf16[16,2,8192]{2,1,0:T(2,128)(2,1)S(1)}, u32[]{:S(2)}, u32[]{:S(2)}) async-start(bf16[16,2,8192]{2,1,0:T(2,128)(2,1)} %reshape.412), calls=%async_computation | async-start | bytes 1048576 | tf_op jit(solution)/shard_map/all_to_all | solution.py:291
  127.8 67.7 %reduce-scatter.5.cloned.1.call-start = ((), (), s32[]{:S(2)}) async-start(), calls=%async_computation.4 | async-start | bytes 2228224 | tf_op jit(solution)/shard_map/reduce_scatter | solution.py:294
  127.8 1.8 copy-start.16
  128.0 1.0 copy-start.7
  132.5 127.8 %reduce-scatter.3.cloned.1.call-start = ((), (), s32[]{:S(2)}) async-start(), calls=%async_computation.3 | async-start | bytes 2228224 | tf_op jit(solution)/shard_map/reduce_scatter | solution.py:316
  142.9 0.8 copy-start.10
  142.9 4.9 %copy-start.6 = (bf16[32,8,16,64]{3,2,1,0:T(8,128)(2,1)S(1)}, bf16[32,8,16,64]{3,2,1,0:T(8,128)(2,1)}, u32[]{:S(2)}) copy-start(bf16[32,8,16,64]{3,2,1,0:T(8,128)(2,1)} %copy-done.5) | copy-start | bytes 1572868
  146.1 2.4 copy-start.20
  146.1 2.4 copy-start.30
  147.8 1.7 copy-start.28
  149.5 1.3 copy-start.4
  150.7 1.3 copy-start.3
  157.9 1.9 copy-start.13
  157.9 2.0 copy-start.17
  157.9 2.0 copy-start.25
  162.6 1.0 copy-start.2
  162.6 1.4 copy-start.8
  162.6 3.7 %copy-start.18 = (bf16[32,16,1536]{2,1,0:T(8,128)(2,1)S(1)}, bf16[32,16,1536]{2,1,0:T(8,128)(2,1)}, u32[]{:S(2)}) copy-start(bf16[32,16,1536]{2,1,0:T(8,128)(2,1)} %reshape.389) | copy-start | bytes 4718596
  166.3 2.6 copy-start.11
Sparse Core Ops, SparseCore 0:
  132.6 62.8 reduce-scatter.4
  199.7 60.5 reduce-scatter.2
